TPU v7x, 512 devices: a whole 4x8x8 slice. The times are simulated.
512 devices in a mesh: dp: 16 (over y, core), comp: 32 (over z, x).
Axes of the slice: x: 4, y: 8, z: 8, core: 2. Of those that a mesh axis runs over, the one named last changes fastest.
Arguments:
- descriptors: bfloat16 [65536, 256], P('dp'), may hold values from -12 to 12
- means: float32 [16384, 256], P('comp'), may hold values from -3 to 3
- variances: float32 [16384, 256], P('comp'), may hold values from 0.5 to 2
- log_weights: float32 [16384], P('comp'), may hold values from -2 to 2
Outputs:
- new_log_weights: float32 [16384], P('comp')
- new_means: float32 [16384, 256], P('comp')
- new_variances: float32 [16384, 256], P('comp')
All inputs are finite; a program needn't handle non-finite values.
Results may differ from a plain program's by a relative error of at most 0.002.
Values sent between devices are 32-bit elements; how exact they have to be, the bound alone decides.
No kernel may reach another device: no remote copies, remote signals or barrier semaphores. Data moves between devices by JAX's collectives and lax.ppermute only.
A program may use at most 64 MiB of HBM per device.

v0:
```python
import jax
import jax.numpy as jnp
from jax import lax
from jax.sharding import PartitionSpec as P

prior_count = 1.0
log_two_pi = 1.8378770664093453


def finish(moments, counts, means, variances, grand_total):
    feature_width = means.shape[1]
    weight = counts + prior_count
    new_means = (moments[:, :feature_width] + prior_count * means) / weight[:, None]
    new_variances = (
        moments[:, feature_width:] + prior_count * (variances + means * means)
    ) / weight[:, None] - new_means * new_means
    new_log_weights = jnp.log(weight) - jnp.log(grand_total)
    return (new_log_weights, new_means, new_variances)


def on_device(descriptors, means, variances, log_weights):
    row_count = descriptors.shape[0]
    feature_width = descriptors.shape[1]
    owned_count = means.shape[0]
    grand_total = row_count * lax.axis_size("dp") + prior_count * owned_count * lax.axis_size(
        "comp"
    )
    precision = 1.0 / variances
    scaled_means = means * precision
    loading = jnp.concatenate([-0.5 * precision, scaled_means], axis=1)
    offset = log_weights - 0.5 * jnp.sum(
        means * scaled_means + jnp.log(variances) + log_two_pi, axis=1
    )
    block_rows = min(512, row_count)
    stacked = descriptors.reshape(row_count // block_rows, block_rows, feature_width)

    def score_block(row_block):
        exact = row_block.astype(jnp.float32)
        features = jnp.concatenate([exact * exact, exact], axis=1)
        return (
            lax.dot_general(
                features,
                loading,
                (((1,), (1,)), ((), ())),
                precision=lax.Precision.HIGHEST,
                preferred_element_type=jnp.float32,
            )
            + offset[None, :]
        )

    scores = lax.map(score_block, stacked).reshape(row_count, owned_count)
    row_max = lax.pmax(jnp.max(scores, axis=1), "comp")
    row_sum = lax.psum(jnp.sum(jnp.exp(scores - row_max[:, None]), axis=1), "comp")
    log_total = row_max + jnp.log(row_sum)
    responsibility = jnp.exp(scores - log_total[:, None])
    counts = jnp.sum(responsibility, axis=0)
    resp_half = responsibility.astype(jnp.bfloat16)
    exact_rows = descriptors.astype(jnp.float32)
    halves = jnp.concatenate([descriptors, (exact_rows * exact_rows).astype(jnp.bfloat16)], axis=1)
    moments = lax.dot_general(
        resp_half, halves, (((0,), (0,)), ((), ())), preferred_element_type=jnp.float32
    )
    summed_moments, summed_counts = lax.psum((moments, counts), "dp")
    new_log_weights, new_means, new_variances = finish(
        summed_moments, summed_counts, means, variances, grand_total
    )
    return (new_log_weights, new_means, new_variances)


def solution(mesh):
    placed = (P("dp", None), P("comp", None), P("comp", None), P("comp"))
    return jax.shard_map(
        on_device,
        mesh=mesh,
        in_specs=placed,
        out_specs=(P("comp"), P("comp", None), P("comp", None)),
        check_vma=False,
    )
```

profile of v0, /device:TPU:1, one launch (start us, length us, event | category | flops | bytes accessed | tf_op | source)
XLA Modules:
  0.0 460.0 jit_solution(11352308650413129347)
XLA Ops:
  7.2 0.0 copy-start
  7.2 0.0 copy-start.4
  7.2 0.0 all-reduce.2.cloned.1.call-start
  7.2 3.5 multiply_convert_fusion
  10.8 1.5 add_reduce_fusion
  12.2 0.1 pad_maximum_fusion
  12.4 0.0 copy-done.4
  12.4 0.0 copy-done
  12.4 23.7 %while.10 = (s32[]{:T(128)}, f32[8,512,512]{2,1,0:T(8,128)}, bf16[8,512,256]{2,1,0:T(8,128)(2,1)S(1)}, f32[512,512]{1,0:T(8,128)S(1)}, f32[512]{0:T(512)S(1)}, /*index=5*/s32[]{:T(128)}) while((s32[]{:T(128)}, f32[8,512,512]{2,1,0:T(8,128)}, bf16[8,512,256]{2,1,0:T(8,128)(2,1)S(1)}, f32[512,512]{1,0:T(8,128)S(1)}, f32[512]{0:T(512)S(1)}, ...), condition=%wide.region_2.3_spmd, body=%wide.region_1.2_spmd.sunk | while | flops 1611530240 | bytes 4721229 | solution.py:51
  12.5 2.9 fusion.28
  15.5 2.9 fusion.28
  18.5 2.9 fusion.28
  21.4 2.9 fusion.28
  24.4 2.8 fusion.28
  27.3 2.9 fusion.28
  30.3 2.9 fusion.28
  33.3 2.8 fusion.28
  36.1 4.0 reduce_max.11
  40.2 121.8 %pmax.7 = f32[4096]{0:T(1024)S(1)} all-reduce(f32[4096]{0:T(1024)S(1)} %bitcast.34), channel_id=1, replica_groups=mesh['dp'=16,'comp'=32] {'comp'}, use_global_device_ids=true, to_apply=%region_4.5 | all-reduce | flops 4096 | bytes 32768 | tf_op jit(solution)/shard_map/pmax | solution.py:52
  162.0 4.4 exponential_reduce_fusion.1
  166.4 110.4 %psum.21 = f32[4096]{0:T(1024)S(1)} all-reduce(f32[4096]{0:T(1024)S(1)} %bitcast.35), channel_id=1, replica_groups=mesh['dp'=16,'comp'=32] {'comp'}, use_global_device_ids=true, to_apply=%region_6.7 | all-reduce | flops 4096 | bytes 32768 | tf_op jit(solution)/shard_map/psum | solution.py:53
  276.8 0.0 copy-start.1
  276.8 4.2 fusion.8
  281.1 0.0 copy-done.1
  281.1 3.3 fusion.9
  284.4 0.0 copy-start.2
  284.4 0.0 copy-start.3
  284.4 0.0 all-reduce.2.cloned.1.call-update
  284.5 4.2 exponential_reduce_fusion
  288.6 79.3 %psum.22 = f32[512]{0:T(512)S(1)} all-reduce(f32[512]{0:T(512)S(1)} %exponential_reduce_fusion), channel_id=1, replica_groups=mesh['dp'=16,'comp'=32] {'dp'}, use_global_device_ids=true, to_apply=%region_8.9 | all-reduce | flops 512 | bytes 4096 | tf_op jit(solution)/shard_map/psum | solution.py:63
  368.0 0.6 broadcast_add_fusion
  368.6 82.2 %all-reduce.2.cloned.1.call-done = f32[512,512]{1,0:T(8,128)} async-done(((f32[512,512]{1,0:T(8,128)}), f32[512,512]{1,0:T(8,128)}) %all-reduce.2.cloned.1.call-update) | async-done | bytes 1048592 | tf_op jit(solution)/shard_map/psum | solution.py:63
  450.8 0.0 copy-done.2
  450.8 0.0 copy-done.3
  450.8 2.4 fusion.14
  (23 shorter events, 0.7 us)
Async XLA Ops:
  7.2 5.3 %copy-start = (bf16[4096,256]{1,0:T(8,128)(2,1)S(1)}, bf16[4096,256]{1,0:T(8,128)(2,1)}, u32[]{:S(2)}) copy-start(bf16[4096,256]{1,0:T(8,128)(2,1)} %param.6) | copy-start | bytes 6291460
  7.2 5.2 %copy-start.4 = (f32[512]{0:T(512)S(1)}, f32[512]{0:T(512)}, u32[]{:S(2)}) copy-start(f32[512]{0:T(512)} %param.9) | copy-start | bytes 6148
  7.2 443.6 %all-reduce.2.cloned.1.call-start = ((), (), s32[]{:S(2)}) async-start(), calls=%async_computation | async-start | bytes 2097152 | tf_op jit(solution)/shard_map/psum | solution.py:63
  276.8 4.3 copy-start.1
  284.4 166.3 %copy-start.2 = (f32[512,256]{1,0:T(8,128)S(1)}, f32[512,256]{1,0:T(8,128)}, u32[]{:S(2)}) copy-start(f32[512,256]{1,0:T(8,128)} %param.8) | copy-start | bytes 1572868
  284.4 166.3 %copy-start.3 = (f32[512,256]{1,0:T(8,128)S(1)}, f32[512,256]{1,0:T(8,128)}, u32[]{:S(2)}) copy-start(f32[512,256]{1,0:T(8,128)} %param.7) | copy-start | bytes 1572868
Sparse Core Ops, SparseCore 0:
  284.6 166.1 all-reduce.1
where the time goes:
time: 460 us
  blocking collectives  312 us (68%)
  waiting for transfers between devices  82.2 us (18%)
  matrix products  26.3 us (6%)
  other arithmetic  25.6 us (6%)
  between operations  14.1 us (3%)
    pmax x1, blocking collectives, on_device(): row_max = lax.pmax(jnp.max(scores, axis=1), 'comp')  122 us
    psum x1, blocking collectives, on_device(): lax.psum(jnp.sum(jnp.exp(scores - row_max[:, None]), axis=1), 'comp')  110 us
    psum x1, waiting for transfers between devices, on_device(): summed_moments, summed_counts = lax.psum((moments, counts), 'dp')  82.2 us
    psum x1, blocking collectives, on_device(): summed_moments, summed_counts = lax.psum((moments, counts), 'dp')  79.3 us
    dot_general x8, matrix products, score_block(): lax.dot_general(features, loading, (((1,), (1,)), ((), ())), precision=la...  22.9 us
  transfers between devices with their start and end apart: 1, of which 1 were waited for; matrix products, arithmetic and copies ran while one was open for 1% of the time, Pallas kernels for 0%

commit v1 on v0

--- a/solution.py
+++ b/solution.py
@@ -50,7 +50,9 @@
 
     scores = lax.map(score_block, stacked).reshape(row_count, owned_count)
     row_max = lax.pmax(jnp.max(scores, axis=1), "comp")
-    row_sum = lax.psum(jnp.sum(jnp.exp(scores - row_max[:, None]), axis=1), "comp")
+    row_sum = jnp.sum(
+        lax.all_gather(jnp.sum(jnp.exp(scores - row_max[:, None]), axis=1), "comp"), axis=0
+    )
     log_total = row_max + jnp.log(row_sum)
     responsibility = jnp.exp(scores - log_total[:, None])
     counts = jnp.sum(responsibility, axis=0)

time: 460 us -> 373 us (0.81)
  blocking collectives: 312 us -> 220 us
    psum x1 -> x0, blocking collectives: 110 us -> none  [on_device(): lax.psum(jnp.sum(jnp.exp(scores - row_max[:, None]), axis=1), 'comp')]
    all_gather x0 -> x1, blocking collectives: none -> 35.1 us  [on_device(): lax.all_gather(jnp.sum(jnp.exp(scores - row_max[:, None]), axis=1), 'comp')]
    psum x1, blocking collectives: 79.3 us -> 63.1 us  [on_device(): summed_moments, summed_counts = lax.psum((moments, counts), 'dp')]
where the time goes in v1:
time: 373 us; the launch traced here: 372 us
  blocking collectives  220 us (59%)
  waiting for transfers between devices  85.7 us (23%)
  matrix products  26.3 us (7%)
  other arithmetic  25.9 us (7%)
  between operations  14.2 us (4%)
    pmax x1, blocking collectives, on_device(): row_max = lax.pmax(jnp.max(scores, axis=1), 'comp')  122 us
    psum x1, waiting for transfers between devices, on_device(): summed_moments, summed_counts = lax.psum((moments, counts), 'dp')  85.7 us
    psum x1, blocking collectives, on_device(): summed_moments, summed_counts = lax.psum((moments, counts), 'dp')  63.1 us
    all_gather x1, blocking collectives, on_device(): lax.all_gather(jnp.sum(jnp.exp(scores - row_max[:, None]), axis=1), 'comp')  35.1 us
    dot_general x8, matrix products, score_block(): lax.dot_general(features, loading, (((1,), (1,)), ((), ())), precision=la...  22.9 us
  transfers between devices with their start and end apart: 1, of which 1 were waited for; matrix products, arithmetic and copies ran while one was open for 1% of the time, Pallas kernels for 0%

profile of v1, /device:TPU:1, one launch (start us, length us, event | category | flops | bytes accessed | tf_op | source)
XLA Modules:
  0.0 372.4 jit_solution(17839552868517572873)
XLA Ops:
  7.2 0.0 copy-start
  7.2 0.0 copy-start.4
  7.2 0.0 all-reduce.2.cloned.1.call-start
  7.2 3.5 multiply_convert_fusion
  10.8 1.5 add_reduce_fusion
  12.2 0.1 pad_maximum_fusion
  12.4 0.0 copy-done.4
  12.4 0.0 copy-done
  12.4 23.7 %while.10 = (s32[]{:T(128)}, f32[8,512,512]{2,1,0:T(8,128)}, bf16[8,512,256]{2,1,0:T(8,128)(2,1)S(1)}, f32[512,512]{1,0:T(8,128)S(1)}, f32[512]{0:T(512)S(1)}, /*index=5*/s32[]{:T(128)}) while((s32[]{:T(128)}, f32[8,512,512]{2,1,0:T(8,128)}, bf16[8,512,256]{2,1,0:T(8,128)(2,1)S(1)}, f32[512,512]{1,0:T(8,128)S(1)}, f32[512]{0:T(512)S(1)}, ...), condition=%wide.region_2.3_spmd, body=%wide.region_1.2_spmd.sunk | while | flops 1611530240 | bytes 4721229 | solution.py:51
  12.5 2.9 fusion.28
  15.5 2.9 fusion.28
  18.5 2.9 fusion.28
  21.4 2.9 fusion.28
  24.4 2.8 fusion.28
  27.3 2.9 fusion.28
  30.3 2.9 fusion.28
  33.3 2.8 fusion.28
  36.1 4.0 %reduce_max.11 = f32[8,512]{1,0:T(8,128)S(1)} reduce(f32[8,512,512]{2,1,0:T(8,128)} %get-tuple-element.30, f32[]{:T(128)} %constant.10.clone.1), dimensions={2}, to_apply=%region_3.4 | reduce | flops 2093056 | bytes 8404996 | tf_op jit(solution)/shard_map/reduce_max | solution.py:52
  40.2 121.8 %pmax.7 = f32[4096]{0:T(1024)S(1)} all-reduce(f32[4096]{0:T(1024)S(1)} %bitcast.31), channel_id=1, replica_groups=mesh['dp'=16,'comp'=32] {'comp'}, use_global_device_ids=true, to_apply=%region_4.5 | all-reduce | flops 4096 | bytes 32768 | tf_op jit(solution)/shard_map/pmax | solution.py:52
  162.0 4.4 %exponential_reduce_fusion.1 = f32[8,512]{1,0:T(8,128)S(1)} fusion(f32[8,512,512]{2,1,0:T(8,128)} %get-tuple-element.30, f32[8,512]{1,0:T(8,128)S(1)} %sub.37), kind=kLoop, calls=%fused_computation.13 | loop fusion | flops 4190208 | bytes 8421376 | tf_op jit(solution)/shard_map/reduce_sum | solution.py:54
  166.4 35.1 %all-gather = f32[32,1,4096]{2,1,0:T(1,128)S(1)} all-gather(f32[1,1,4096]{2,1,0:T(1,128)S(1)} %reshape.34), channel_id=1, replica_groups=mesh['dp'=16,'comp'=32] {'comp'}, dimensions={0}, use_global_device_ids=true | all-gather | bytes 540672 | tf_op jit(solution)/shard_map/all_gather | solution.py:54
  201.6 0.4 reduce_sum.38
  201.9 0.0 copy-start.1
  201.9 4.2 %fusion.8 = bf16[4096,512]{1,0:T(8,128)(2,1)S(1)} fusion(f32[8,512,512]{2,1,0:T(8,128)} %get-tuple-element.30, f32[4096]{0:T(1024)S(1)} %log_add_fusion), kind=kLoop, calls=%fused_computation.11 | loop fusion | flops 4194304 | bytes 12599296 | tf_op jit(solution)/shard_map/convert_element_type | solution.py:59
  206.2 0.0 copy-done.1
  206.2 3.3 fusion.9
  209.5 0.0 copy-start.2
  209.5 0.0 copy-start.3
  209.5 0.0 all-reduce.2.cloned.1.call-update
  209.6 4.2 %exponential_reduce_fusion = f32[512]{0:T(512)S(1)} fusion(f32[8,512,512]{2,1,0:T(8,128)} %get-tuple-element.30, f32[8,512]{1,0:T(8,128)S(1)} %sub.40), kind=kLoop, calls=%fused_computation.12 | loop fusion | flops 4193792 | bytes 8407040 | tf_op jit(solution)/shard_map/reduce_sum | solution.py:58
  213.7 63.1 %psum.14 = f32[512]{0:T(512)S(1)} all-reduce(f32[512]{0:T(512)S(1)} %exponential_reduce_fusion), channel_id=1, replica_groups=mesh['dp'=16,'comp'=32] {'dp'}, use_global_device_ids=true, to_apply=%region_8.9 | all-reduce | flops 512 | bytes 4096 | tf_op jit(solution)/shard_map/psum | solution.py:65
  276.9 0.6 broadcast_add_fusion
  277.5 85.7 %all-reduce.2.cloned.1.call-done = f32[512,512]{1,0:T(8,128)} async-done(((f32[512,512]{1,0:T(8,128)}), f32[512,512]{1,0:T(8,128)}) %all-reduce.2.cloned.1.call-update) | async-done | bytes 1048592 | tf_op jit(solution)/shard_map/psum | solution.py:65
  363.2 0.0 copy-done.2
  363.2 0.0 copy-done.3
  363.2 2.4 fusion.14
  (23 shorter events, 0.7 us)
Async XLA Ops:
  7.2 5.3 %copy-start = (bf16[4096,256]{1,0:T(8,128)(2,1)S(1)}, bf16[4096,256]{1,0:T(8,128)(2,1)}, u32[]{:S(2)}) copy-start(bf16[4096,256]{1,0:T(8,128)(2,1)} %param.6) | copy-start | bytes 6291460
  7.2 5.2 %copy-start.4 = (f32[512]{0:T(512)S(1)}, f32[512]{0:T(512)}, u32[]{:S(2)}) copy-start(f32[512]{0:T(512)} %param.9) | copy-start | bytes 6148
  7.2 356.0 %all-reduce.2.cloned.1.call-start = ((), (), s32[]{:S(2)}) async-start(), calls=%async_computation | async-start | bytes 2097152 | tf_op jit(solution)/shard_map/psum | solution.py:65
  201.9 4.3 %copy-start.1 = (bf16[4096,256]{1,0:T(8,128)(2,1)S(1)}, bf16[4096,256]{1,0:T(8,128)(2,1)}, u32[]{:S(2)}) copy-start(bf16[4096,256]{1,0:T(8,128)(2,1)} %multiply_convert_fusion) | copy-start | bytes 6291460
  209.5 153.7 %copy-start.2 = (f32[512,256]{1,0:T(8,128)S(1)}, f32[512,256]{1,0:T(8,128)}, u32[]{:S(2)}) copy-start(f32[512,256]{1,0:T(8,128)} %param.8) | copy-start | bytes 1572868
  209.5 153.7 %copy-start.3 = (f32[512,256]{1,0:T(8,128)S(1)}, f32[512,256]{1,0:T(8,128)}, u32[]{:S(2)}) copy-start(f32[512,256]{1,0:T(8,128)} %param.7) | copy-start | bytes 1572868
Sparse Core Ops, SparseCore 0:
  209.7 153.4 all-reduce.1
